TPU v7x, 256 devices: a whole 4x4x8 slice. The times are simulated.
256 devices in a mesh: req: 32 (over x, z), tp: 8 (over y, core).
Axes of the slice: x: 4, y: 4, z: 8, core: 2. Of those that a mesh axis runs over, the one named last changes fastest.
Arguments:
- hidden: bfloat16 [4096, 2048], P('req', 'tp'), may hold values from -3 to 3
- lengths: int32 [4096], P('req'), may hold values from 1 to 1921, as said below
- routes: int32 [4096, 6], P('req'), may hold values from 0 to 63, all different within a row; in each aligned block of 128 rows (0 to 127, 128 to 255, ...) at most 32 rows name the same one
- latent_cache: bfloat16 [65536, 576], P('req'), may hold values from -400 to 400
- attention_gain: bfloat16 [2048], replicated, may hold values from 0.099609375 to 1.8984375
- query_weight: bfloat16 [2048, 3072], P(None, 'tp'), may hold values from -0.125 to 0.125
- latent_weight: bfloat16 [2048, 576], P(None, 'tp'), may hold values from -0.125 to 0.125
- latent_gain: bfloat16 [512], replicated, may hold values from 0.099609375 to 1.8984375
- key_absorb: bfloat16 [16, 128, 512], P('tp'), may hold values from -0.5 to 0.5
- value_absorb: bfloat16 [16, 512, 128], P('tp'), may hold values from -0.5 to 0.5
- output_weight: bfloat16 [2048, 2048], P('tp'), may hold values from -0.75 to 0.75
- feedforward_gain: bfloat16 [2048], replicated, may hold values from 0.099609375 to 1.8984375
- router_weight: bfloat16 [2048, 64], replicated, may hold values from -0.0625 to 0.0625
- expert_gate: bfloat16 [64, 2048, 1408], P('req', None, 'tp'), may hold values from -0.25 to 0.25
- expert_up: bfloat16 [64, 2048, 1408], P('req', None, 'tp'), may hold values from -0.25 to 0.25
- expert_down: bfloat16 [64, 1408, 2048], P('req', 'tp'), may hold values from -0.4375 to 0.4375
- shared_gate: bfloat16 [2048, 1408], P(None, 'tp'), may hold values from -0.25 to 0.25
- shared_up: bfloat16 [2048, 1408], P(None, 'tp'), may hold values from -0.25 to 0.25
- shared_down: bfloat16 [1408, 2048], P('tp'), may hold values from -0.21875 to 0.21875
Outputs:
- next_hidden: bfloat16 [4096, 2048], P('req', 'tp')
- new_rows: bfloat16 [4096, 576], P('req')
Inputs may be any that keep to these rules, and one draw needn't show every extreme that they name: The lengths of the 128 requests of one index of req (aligned blocks of 128) sum to at most 2048, and to exactly 2048 on some index, where one request holds 1921. `routes`: among the rows of one index of req, no expert is named by more than 32 rows, a bound that some block reaches.
All inputs are finite; a program needn't handle non-finite values.
Results may differ from a plain program's by a relative error of at most 0.023.
The roundings to bfloat16 on the way count: a program that leaves them out, or rounds other values in their place, can miss the bound.
Values may be sent and summed in bfloat16 or wider, within the bound.
No kernel may reach another device: no remote copies, remote signals or barrier semaphores. Data moves between devices by JAX's collectives and lax.ppermute only.
A program may use at most 128 MiB of HBM per device.

v0:
```python
import jax
import jax.numpy as jnp
from jax import lax
from jax.sharding import PartitionSpec as P

rope_base = 50000.0
route_scale = 2.446
norm_eps = 1e-06


def rms_norm(values, gains):
    widened = values.astype(jnp.float32)
    factor = lax.rsqrt(jnp.mean(widened * widened, axis=-1, keepdims=True) + norm_eps)
    return widened * factor * gains.astype(jnp.float32)


def rotate(values, positions):
    half_width = values.shape[-1] // 2
    exponent = jnp.arange(half_width, dtype=jnp.float32) * (2.0 / values.shape[-1])
    angles = positions[..., None] * jnp.power(rope_base, -exponent)
    cosine = jnp.cos(angles)
    sine_part = jnp.sin(angles)
    first_half = values[..., :half_width]
    second_half = values[..., half_width:]
    return jnp.concatenate(
        [
            first_half * cosine - second_half * sine_part,
            first_half * sine_part + second_half * cosine,
        ],
        axis=-1,
    )


def attend(queries, cache_rows, lengths, new_rows, score_scale, latent_width):
    starts = jnp.cumsum(lengths) - lengths
    places = jnp.arange(cache_rows.shape[0], dtype=jnp.int32)
    inside = (places[None, :] >= starts[:, None]) & (places[None, :] < (starts + lengths)[:, None])
    scores = (
        jnp.einsum("rhk,jk->rhj", queries, cache_rows, preferred_element_type=jnp.float32)
        * score_scale
    )
    own_score = (
        jnp.einsum("rhk,rk->rh", queries, new_rows, preferred_element_type=jnp.float32)
        * score_scale
    )
    highest = jnp.maximum(
        jnp.max(jnp.where(inside[:, None, :], scores, -jnp.inf), axis=-1), own_score
    )
    weights = jnp.where(inside[:, None, :], jnp.exp(scores - highest[..., None]), 0.0)
    own_weight = jnp.exp(own_score - highest)
    totals = jnp.sum(weights, axis=-1) + own_weight
    probabilities = (weights / totals[..., None]).astype(jnp.bfloat16)
    own_prob = (own_weight / totals).astype(jnp.bfloat16)
    summed = jnp.einsum(
        "rhj,jl->rhl",
        probabilities,
        cache_rows[:, :latent_width],
        preferred_element_type=jnp.float32,
    )
    summed = summed + own_prob.astype(jnp.float32)[..., None] * new_rows[
        :, None, :latent_width
    ].astype(jnp.float32)
    return summed.astype(jnp.bfloat16)


def shards(
    hidden,
    lengths,
    routes,
    latent_cache,
    attention_gain,
    query_weight,
    latent_weight,
    latent_gain,
    key_absorb,
    value_absorb,
    output_weight,
    feedforward_gain,
    router_weight,
    expert_gate,
    expert_up,
    expert_down,
    shared_gate,
    shared_up,
    shared_down,
):
    token_count = hidden.shape[0]
    owner_count = lax.axis_size("req")
    column_width = hidden.shape[1]
    column_start = lax.axis_index("tp") * column_width
    heads_here = key_absorb.shape[0]
    nope_width = key_absorb.shape[1]
    latent_width = key_absorb.shape[2]
    whole = lax.all_gather(hidden, "tp", axis=1, tiled=True)
    normed = rms_norm(whole, attention_gain).astype(jnp.bfloat16)
    projected = jnp.dot(normed, query_weight, preferred_element_type=jnp.float32).reshape(
        token_count, heads_here, -1
    )
    rope_width = projected.shape[2] - nope_width
    positions = lengths.astype(jnp.float32)
    query_nope = projected[..., :nope_width].astype(jnp.bfloat16)
    query_rope = rotate(projected[..., nope_width:], positions[:, None]).astype(jnp.bfloat16)
    query_latent = jnp.einsum(
        "thn,hnl->thl", query_nope, key_absorb, preferred_element_type=jnp.float32
    ).astype(jnp.bfloat16)
    latent_part = jnp.dot(normed, latent_weight, preferred_element_type=jnp.float32).astype(
        jnp.bfloat16
    )
    latent_raw = lax.all_gather(latent_part, "tp", axis=1, tiled=True)
    latent_new = rms_norm(latent_raw[:, :latent_width], latent_gain)
    key_new = rotate(latent_raw[:, latent_width:].astype(jnp.float32), positions)
    new_rows = jnp.concatenate([latent_new, key_new], axis=-1).astype(jnp.bfloat16)
    queries = jnp.concatenate([query_latent, query_rope], axis=-1)
    attended = attend(
        queries, latent_cache, lengths, new_rows, (nope_width + rope_width) ** (-0.5), latent_width
    )
    head_values = jnp.einsum(
        "thl,hlv->thv", attended, value_absorb, preferred_element_type=jnp.float32
    ).astype(jnp.bfloat16)
    attention = jnp.dot(
        head_values.reshape(token_count, -1), output_weight, preferred_element_type=jnp.float32
    )
    total_attention = lax.psum(attention, "tp")
    mixed = (whole.astype(jnp.float32) + total_attention).astype(jnp.bfloat16)
    mixed_columns = lax.dynamic_slice_in_dim(mixed, column_start, column_width, 1)
    expert_in = rms_norm(mixed, feedforward_gain).astype(jnp.bfloat16)
    logits = jnp.dot(expert_in, router_weight, preferred_element_type=jnp.float32)
    expert_count = router_weight.shape[1]
    top_count = routes.shape[1]
    per_owner = expert_count // owner_count
    slot_count = max(2, 8 * token_count * top_count // (3 * expert_count))
    chosen = jnp.take_along_axis(jax.nn.sigmoid(logits), routes, axis=1)
    route_weights = chosen / jnp.sum(chosen, axis=1, keepdims=True) * route_scale
    expert_ids = routes.reshape(-1)
    onehot = (expert_ids[:, None] == jnp.arange(expert_count, dtype=jnp.int32)[None, :]).astype(
        jnp.int32
    )
    earlier = jnp.cumsum(onehot, axis=0) - onehot
    slot_index = jnp.sum(earlier * onehot, axis=1)
    slot_places = (expert_ids * slot_count + slot_index).reshape(token_count, top_count)
    slot_total = expert_count * slot_count
    placed = slot_places[None, :, :] == jnp.arange(slot_total, dtype=jnp.int32)[:, None, None]
    gather_matrix = jnp.any(placed, axis=2).astype(jnp.bfloat16)
    combine_matrix = jnp.sum(jnp.where(placed, route_weights[None, :, :], 0.0), axis=2).T
    outgoing = jnp.dot(gather_matrix, expert_in, preferred_element_type=jnp.float32).astype(
        jnp.bfloat16
    )
    outgoing = outgoing.reshape(owner_count, per_owner, slot_count, expert_in.shape[1])
    slab = lax.all_to_all(outgoing, "req", split_axis=0, concat_axis=0, tiled=True)
    gate_part = jnp.einsum("oesd,edf->oesf", slab, expert_gate, preferred_element_type=jnp.float32)
    up_part = jnp.einsum("oesd,edf->oesf", slab, expert_up, preferred_element_type=jnp.float32)
    inner_units = (jax.nn.silu(gate_part) * up_part).astype(jnp.bfloat16)
    partial_out = jnp.einsum(
        "oesf,efd->oesd", inner_units, expert_down, preferred_element_type=jnp.float32
    )
    results = lax.psum_scatter(partial_out, "tp", scatter_dimension=3, tiled=True)
    shared_inner = (
        jax.nn.silu(jnp.dot(expert_in, shared_gate, preferred_element_type=jnp.float32))
        * jnp.dot(expert_in, shared_up, preferred_element_type=jnp.float32)
    ).astype(jnp.bfloat16)
    shared_part = jnp.dot(shared_inner, shared_down, preferred_element_type=jnp.float32)
    returned = lax.all_to_all(results, "req", split_axis=0, concat_axis=0, tiled=True)
    routed = jnp.dot(
        combine_matrix, returned.reshape(slot_total, column_width), precision=lax.Precision.HIGHEST
    )
    shared_columns = lax.psum_scatter(shared_part, "tp", scatter_dimension=1, tiled=True)
    next_hidden = (mixed_columns.astype(jnp.float32) + routed + shared_columns).astype(jnp.bfloat16)
    return (next_hidden, new_rows)


def solution(mesh):
    in_specs = (
        P("req", "tp"),
        P("req"),
        P("req", None),
        P("req", None),
        P(),
        P(None, "tp"),
        P(None, "tp"),
        P(),
        P("tp", None, None),
        P("tp", None, None),
        P("tp", None),
        P(),
        P(),
        P("req", None, "tp"),
        P("req", None, "tp"),
        P("req", "tp", None),
        P(None, "tp"),
        P(None, "tp"),
        P("tp", None),
    )
    out_specs = (P("req", "tp"), P("req", None))
    return jax.shard_map(shards, mesh=mesh, in_specs=in_specs, out_specs=out_specs, check_vma=False)
```

profile of v0, /device:TPU:1, one launch (start us, length us, event | category | flops | bytes accessed | tf_op | source)
XLA Modules:
  0.0 509.0 jit_solution(7842593407011253523)
XLA Ops:
  7.2 0.0 all-reduce.2.cloned.1.call-start
  7.2 16.5 %all_gather.6 = bf16[128,2048]{1,0:T(8,128)(2,1)S(1)} all-gather(bf16[128,256]{1,0:T(8,128)(2,1)} %param.19), channel_id=1, replica_groups=mesh['req'=32,'tp'=8] {'tp'}, dimensions={1}, use_global_device_ids=true | all-gather | bytes 589824 | tf_op jit(solution)/shard_map/all_gather | solution.py:94
  23.7 0.2 fusion.45
  23.9 0.7 convert_element_type.92
  24.6 1.3 convolution_convert_fusion.2
  26.0 12.8 %all_gather.7 = bf16[128,576]{0,1:T(8,128)(2,1)S(1)} all-gather(bf16[128,72]{0,1:T(8,128)(2,1)S(1)} %convolution_convert_fusion.2), channel_id=1, replica_groups=mesh['req'=32,'tp'=8] {'tp'}, dimensions={1}, use_global_device_ids=true | all-gather | bytes 165888 | tf_op jit(solution)/shard_map/all_gather | solution.py:109
  38.7 0.1 fusion.60
  38.9 0.1 copy.105
  39.0 0.2 reduce-window.18
  39.2 0.1 reduce.1
  39.3 0.5 copy-done.8
  39.8 0.5 fusion.94
  40.3 0.1 fusion.62
  40.5 0.8 copy.114
  41.3 0.1 subtract_convert_fusion.1
  41.5 0.1 copy.140
  41.7 0.7 copy.109
  42.4 0.7 copy.111
  43.1 0.8 fusion.70
  43.9 0.1 copy.137
  44.0 0.1 copy.138
  44.1 0.3 fusion.31
  44.4 1.1 fusion.56
  45.5 0.9 subtract_convert_fusion
  46.4 0.2 multiply_reduce_fusion
  46.6 2.9 select_reduce_fusion.1
  49.5 1.3 copy-done.2
  50.9 0.6 fusion.13
  51.4 3.5 fusion.34
  55.0 1.4 fusion.95
  56.4 0.0 reduce-scatter.3.cloned.1.call-start
  56.4 0.1 copy.116
  56.5 0.1 eq.42
  56.7 0.1 eq.38
  56.9 1.8 reduce-window.19
  58.7 0.3 slice_reduce_fusion
  59.0 0.1 fusion.67
  59.1 0.1 reduce_sum.69
  59.2 0.1 copy.119
  59.3 1.1 fusion.4
  60.4 62.6 %all-reduce.2.cloned.1.call-done = f32[128,2048]{1,0:T(8,128)} async-done(((f32[128,2048]{1,0:T(8,128)}), f32[128,2048]{1,0:T(8,128)}) %all-reduce.2.cloned.1.call-update) | async-done | bytes 1048592 | tf_op jit(solution)/shard_map/psum | solution.py:123
  123.0 1.5 fusion.42
  124.4 2.4 convolution_convert_fusion
  126.9 190.3 %all_to_all.10 = bf16[32,2,32,2048]{3,2,1,0:T(8,128)(2,1)S(1)} all-to-all(bf16[32,2,32,2048]{3,2,1,0:T(8,128)(2,1)S(1)} %bitcast.104), channel_id=1, replica_groups=mesh['req'=32,'tp'=8] {'req'}, dimensions={0} | all-to-all | bytes 16777216 | tf_op jit(solution)/shard_map/all_to_all | solution.py:149
  317.2 3.2 copy-done.1
  320.4 3.7 fusion.2
  324.1 15.2 %convolution_bitcast_fusion = f32[32,2,32,2048]{3,2,0,1:T(8,128)} fusion(f32[2,32,32,176]{3,2,1,0:T(8,128)} %fusion.2, bf16[32,2,32,2048]{3,2,1,0:T(8,128)(2,1)} %copy-done.1, bf16[2,176,2048]{2,1,0:T(8,128)(2,1)} %param.34, bf16[2,2048,176]{1,2,0:T(8,128)(2,1)} %param.33), kind=kOutput, calls=%fused_computation.6 | convolution fusion | flops 2954952704 | bytes 29491200 | tf_op jit(solution)/shard_map/oesf,efd->oesd/dot_general | solution.py:153
  339.3 0.0 reduce-scatter.3.cloned.1.call-update
  339.4 96.5 %reduce-scatter.3.cloned.1.call-done = f32[32,2,32,256]{3,2,0,1:T(8,128)} async-done(((f32[32,2,32,2048]{3,2,0,1:T(8,128)}), f32[32,2,32,256]{3,2,0,1:T(8,128)}) %reduce-scatter.3.cloned.1.call-update) | async-done | bytes 2097168 | tf_op jit(solution)/shard_map/reduce_scatter | solution.py:156
  435.8 3.2 copy.124
  439.0 9.8 %all-to-all-start.1 = ((f32[32,2,32,256]{3,2,1,0:T(8,128)}), f32[32,2,32,256]{3,2,1,0:T(8,128)}, u32[]{:S(2)}, u32[]{:S(2)}) async-start(f32[32,2,32,256]{3,2,1,0:T(8,128)} %copy.124), calls=%async_computation.2 | async-start | bytes 4194304 | tf_op jit(solution)/shard_map/all_to_all | solution.py:162
  448.9 0.0 reduce-scatter.5.cloned.1.call-start
  448.9 1.5 fusion.88
  450.5 3.2 fusion.38
  453.7 0.1 copy.120
  453.8 0.1 reshape.227
  453.9 0.4 fusion.41
  454.3 5.1 %gather_fusion = f32[768]{0:T(1024)S(1)} fusion(f32[128,64]{0,1:T(8,128)S(1)} %fusion.41, s32[768]{0:T(1024)S(1)} %reshape.227), kind=kCustom, calls=%fused_computation | custom fusion | bytes 12288 | tf_op jit(solution)/shard_map/jit(take_along_axis)/gather | solution.py:132
  459.4 0.1 reshape.230
  459.6 0.1 copy.121
  459.7 1.8 select_reduce_fusion
  461.5 25.5 %reduce-scatter.5.cloned.1.call-done = f32[128,256]{1,0:T(8,128)} async-done(((f32[128,2048]{1,0:T(8,128)}), f32[128,256]{1,0:T(8,128)}) %reduce-scatter.5.cloned.1.call-update) | async-done | bytes 131088 | tf_op jit(solution)/shard_map/reduce_scatter | solution.py:166
  487.0 11.1 %all-to-all-done.1 = f32[32,2,32,256]{3,2,1,0:T(8,128)} async-done(((f32[32,2,32,256]{3,2,1,0:T(8,128)}), f32[32,2,32,256]{3,2,1,0:T(8,128)}, u32[]{:S(2)}, u32[]{:S(2)}) %all-to-all-start.1) | async-done | bytes 2097184 | tf_op jit(solution)/shard_map/all_to_all | solution.py:162
  498.1 4.3 fusion.33
  (44 shorter events, 0.3 us)
Async XLA Ops:
  7.2 35.9 %copy-start = (bf16[2048,384]{1,0:T(8,128)(2,1)S(1)}, bf16[2048,384]{1,0:T(8,128)(2,1)}, u32[]{:S(2)}) copy-start(bf16[2048,384]{1,0:T(8,128)(2,1)} %param.24) | copy-start | bytes 4718596
  7.2 31.7 %copy-start.11 = (bf16[512]{0:T(512)(128)(2,1)S(1)}, bf16[512]{0:T(512)(128)(2,1)}, u32[]{:S(2)}) copy-start(bf16[512]{0:T(512)(128)(2,1)} %param.26) | copy-start | bytes 3076
  7.2 31.7 %copy-start.10 = (s32[128]{0:T(128)S(1)}, s32[128]{0:T(128)}, u32[]{:S(2)}) copy-start(s32[128]{0:T(128)} %param.20) | copy-start | bytes 1540
  7.2 115.8 %all-reduce.2.cloned.1.call-start = ((), (), s32[]{:S(2)}) async-start(), calls=%async_computation.4 | async-start | bytes 2097152 | tf_op jit(solution)/shard_map/psum | solution.py:123
  39.3 0.6 copy-start.8
  40.5 3.6 copy-start.6
  41.5 4.0 copy-start.5
  49.5 1.4 copy-start.2
  51.4 3.5 copy-start.3
  54.9 1.5 copy-start.7
  55.0 4.3 copy-start.9
  56.4 379.5 %reduce-scatter.3.cloned.1.call-start = ((), (), s32[]{:S(2)}) async-start(), calls=%async_computation.5 | async-start | bytes 18874368 | tf_op jit(solution)/shard_map/reduce_scatter | solution.py:156
  126.9 193.5 %copy-start.12 = (bf16[2,2048,176]{1,2,0:T(8,128)(2,1)S(1)}, bf16[2,2048,176]{1,2,0:T(8,128)(2,1)}, u32[]{:S(2)}) copy-start(bf16[2,2048,176]{1,2,0:T(8,128)(2,1)} %param.32) | copy-start | bytes 4325380
  317.2 3.2 copy-start.1
  439.0 11.4 %copy-start.4 = (bf16[176,2048]{1,0:T(8,128)(2,1)S(1)}, bf16[176,2048]{1,0:T(8,128)(2,1)}, u32[]{:S(2)}) copy-start(bf16[176,2048]{1,0:T(8,128)(2,1)} %param.37) | copy-start | bytes 2162692
  439.0 59.1 %all-to-all-start.1 = ((f32[32,2,32,256]{3,2,1,0:T(8,128)}), f32[32,2,32,256]{3,2,1,0:T(8,128)}, u32[]{:S(2)}, u32[]{:S(2)}) async-start(f32[32,2,32,256]{3,2,1,0:T(8,128)} %copy.124), calls=%async_computation.2 | async-start | bytes 4194304 | tf_op jit(solution)/shard_map/all_to_all | solution.py:162
  448.9 38.1 %reduce-scatter.5.cloned.1.call-start = ((), (), s32[]{:S(2)}) async-start(), calls=%async_computation.6 | async-start | bytes 1179648 | tf_op jit(solution)/shard_map/reduce_scatter | solution.py:166
  450.5 3.5 copy-start.13
Sparse Core Ops, SparseCore 0:
  56.5 66.4 all-reduce.1
  339.5 96.3 reduce-scatter.2
  453.8 33.1 reduce-scatter.4
where the time goes:
time: 510 us; the launch traced here: 509 us
  blocking collectives  220 us (43%)
  waiting for transfers between devices  196 us (38%)
  matrix products  40.9 us (8%)
  local copies, waits for them, and re-layouts  17.5 us (3%)
  between operations  14.1 us (3%)
  other arithmetic  11.2 us (2%)
  starting transfers between devices  9.94 us (2%)
    all_to_all x1, blocking collectives, shards(): lax.all_to_all(outgoing, 'req', split_axis=0, concat_axis=0, tiled=True)  190 us
    reduce_scatter x1, waiting for transfers between devices, shards(): lax.psum_scatter(partial_out, 'tp', scatter_dimension=3, tiled=True)  96.5 us
    psum x1, waiting for transfers between devices, shards(): total_attention = lax.psum(attention, 'tp')  62.6 us
    reduce_scatter x1, waiting for transfers between devices, shards(): lax.psum_scatter(shared_part, 'tp', scatter_dimension=1, tiled=True)  25.5 us
    all_gather x1, blocking collectives, shards(): whole = lax.all_gather(hidden, 'tp', axis=1, tiled=True)  16.5 us
    dot_general x1, matrix products, shards(): jnp.einsum('oesf,efd->oesd', inner_units, expert_down, preferred_element_...  15.2 us
    all_gather x1, blocking collectives, shards(): latent_raw = lax.all_gather(latent_part, 'tp', axis=1, tiled=True)  12.8 us
    all_to_all x1, waiting for transfers between devices, shards(): lax.all_to_all(results, 'req', split_axis=0, concat_axis=0, tiled=True)  11.1 us
  transfers between devices with their start and end apart: 4, of which 4 were waited for; matrix products, arithmetic and copies ran while one was open for 3% of the time, Pallas kernels for 0%

commit v1 on v0

--- a/solution.py
+++ b/solution.py
@@ -120,7 +120,7 @@
     attention = jnp.dot(
         head_values.reshape(token_count, -1), output_weight, preferred_element_type=jnp.float32
     )
-    total_attention = lax.psum(attention, "tp")
+    total_attention = jnp.sum(lax.all_gather(attention, "tp"), axis=0)
     mixed = (whole.astype(jnp.float32) + total_attention).astype(jnp.bfloat16)
     mixed_columns = lax.dynamic_slice_in_dim(mixed, column_start, column_width, 1)
     expert_in = rms_norm(mixed, feedforward_gain).astype(jnp.bfloat16)

time: 510 us -> 493 us (0.967)
  waiting for transfers between devices: 196 us -> 181 us
    psum x1 -> x0, waiting for transfers between devices: 62.6 us -> none  [shards(): total_attention = lax.psum(attention, 'tp')]
    all_gather x0 -> x1, waiting for transfers between devices: none -> 49.3 us  [shards(): total_attention = jnp.sum(lax.all_gather(attention, 'tp'), axis=0)]
where the time goes in v1:
time: 493 us
  blocking collectives  221 us (45%)
  waiting for transfers between devices  181 us (37%)
  matrix products  38.8 us (8%)
  local copies, waits for them, and re-layouts  15 us (3%)
  between operations  14.2 us (3%)
  other arithmetic  12.2 us (2%)
  starting transfers between devices  10.1 us (2%)
    all_to_all x1, blocking collectives, shards(): lax.all_to_all(outgoing, 'req', split_axis=0, concat_axis=0, tiled=True)  192 us
    reduce_scatter x1, waiting for transfers between devices, shards(): lax.psum_scatter(partial_out, 'tp', scatter_dimension=3, tiled=True)  93.1 us
    all_gather x1, waiting for transfers between devices, shards(): total_attention = jnp.sum(lax.all_gather(attention, 'tp'), axis=0)  49.3 us
    reduce_scatter x1, waiting for transfers between devices, shards(): lax.psum_scatter(shared_part, 'tp', scatter_dimension=1, tiled=True)  25.9 us
    all_gather x1, blocking collectives, shards(): whole = lax.all_gather(hidden, 'tp', axis=1, tiled=True)  16.5 us
    dot_general x1, matrix products, shards(): jnp.einsum('oesf,efd->oesd', inner_units, expert_down, preferred_element_...  15.2 us
    all_gather x1, blocking collectives, shards(): latent_raw = lax.all_gather(latent_part, 'tp', axis=1, tiled=True)  12.8 us
    all_to_all x1, waiting for transfers between devices, shards(): lax.all_to_all(results, 'req', split_axis=0, concat_axis=0, tiled=True)  12.7 us
  transfers between devices with their start and end apart: 4, of which 4 were waited for; matrix products, arithmetic and copies ran while one was open for 3% of the time, Pallas kernels for 0%

profile of v1, /device:TPU:1, one launch (start us, length us, event | category | flops | bytes accessed | tf_op | source)
XLA Modules:
  0.0 492.8 jit_solution(14131440028801182680)
XLA Ops:
  7.2 0.0 all-gather.3.cloned.1.call-start
  7.2 16.5 %all_gather.12 = bf16[128,2048]{1,0:T(8,128)(2,1)S(1)} all-gather(bf16[128,256]{1,0:T(8,128)(2,1)} %param.19), channel_id=1, replica_groups=mesh['req'=32,'tp'=8] {'tp'}, dimensions={1}, use_global_device_ids=true | all-gather | bytes 589824 | tf_op jit(solution)/shard_map/all_gather | solution.py:94
  23.7 0.2 fusion.45
  23.9 0.7 convert_element_type.92
  24.6 1.3 convolution_convert_fusion.2
  26.0 12.8 %all_gather.13 = bf16[128,576]{0,1:T(8,128)(2,1)S(1)} all-gather(bf16[128,72]{0,1:T(8,128)(2,1)S(1)} %convolution_convert_fusion.2), channel_id=1, replica_groups=mesh['req'=32,'tp'=8] {'tp'}, dimensions={1}, use_global_device_ids=true | all-gather | bytes 165888 | tf_op jit(solution)/shard_map/all_gather | solution.py:109
  38.7 0.1 fusion.60
  38.9 0.1 copy.105
  39.0 0.2 reduce-window.18
  39.2 0.1 reduce.1
  39.3 0.1 fusion.62
  39.4 0.1 copy.114
  39.6 0.1 subtract_convert_fusion.1
  39.7 0.1 copy.140
  39.9 0.1 copy.109
  40.0 0.1 copy.111
  40.1 0.8 fusion.70
  40.9 0.1 copy.137
  41.0 0.1 copy.138
  41.1 0.3 fusion.31
  41.4 0.5 fusion.56
  41.9 0.2 multiply_reduce_fusion
  42.1 2.9 select_reduce_fusion.1
  45.0 1.3 copy-done.3
  46.3 0.6 fusion.13
  46.9 3.5 fusion.34
  50.4 1.4 fusion.95
  51.8 0.0 all-gather.3.cloned.1.call-update
  51.8 0.0 reduce-scatter.3.cloned.1.call-start
  51.9 0.1 copy.116
  52.0 0.1 eq.42
  52.1 0.1 eq.38
  52.3 1.8 reduce-window.19
  54.1 0.3 slice_reduce_fusion
  54.4 0.1 fusion.67
  54.6 0.1 reduce_sum.79
  54.7 0.1 copy.119
  54.8 1.1 fusion.4
  55.9 49.3 %all-gather.3.cloned.1.call-done = f32[1024,2048]{1,0:T(8,128)} async-done(((f32[128,2048]{1,0:T(8,128)}), f32[1024,2048]{1,0:T(8,128)}) %all-gather.3.cloned.1.call-update) | async-done | bytes 8388624 | tf_op jit(solution)/shard_map/all_gather | solution.py:123
  105.2 4.2 reduce_sum.77
  109.4 0.2 fusion.42
  109.6 2.4 convolution_convert_fusion
  112.1 192.1 %all_to_all.10 = bf16[32,2,32,2048]{3,2,1,0:T(8,128)(2,1)S(1)} all-to-all(bf16[32,2,32,2048]{3,2,1,0:T(8,128)(2,1)S(1)} %bitcast.105), channel_id=1, replica_groups=mesh['req'=32,'tp'=8] {'req'}, dimensions={0} | all-to-all | bytes 16777216 | tf_op jit(solution)/shard_map/all_to_all | solution.py:149
  304.2 3.2 copy-done.2
  307.4 3.8 fusion.2
  311.3 15.2 %convolution_bitcast_fusion = f32[32,2,32,2048]{3,2,0,1:T(8,128)} fusion(f32[2,32,32,176]{3,2,1,0:T(8,128)} %fusion.2, bf16[32,2,32,2048]{3,2,1,0:T(8,128)(2,1)} %copy-done.2, bf16[2,176,2048]{2,1,0:T(8,128)(2,1)} %param.34, bf16[2,2048,176]{1,2,0:T(8,128)(2,1)} %param.33), kind=kOutput, calls=%fused_computation.6 | convolution fusion | flops 2954952704 | bytes 29491200 | tf_op jit(solution)/shard_map/oesf,efd->oesd/dot_general | solution.py:153
  326.5 0.0 reduce-scatter.3.cloned.1.call-update
  326.5 93.1 %reduce-scatter.3.cloned.1.call-done = f32[32,2,32,256]{3,2,0,1:T(8,128)} async-done(((f32[32,2,32,2048]{3,2,0,1:T(8,128)}), f32[32,2,32,256]{3,2,0,1:T(8,128)}) %reduce-scatter.3.cloned.1.call-update) | async-done | bytes 2097168 | tf_op jit(solution)/shard_map/reduce_scatter | solution.py:156
  419.7 3.2 copy.124
  422.9 9.8 %all-to-all-start.1 = ((f32[32,2,32,256]{3,2,1,0:T(8,128)}), f32[32,2,32,256]{3,2,1,0:T(8,128)}, u32[]{:S(2)}, u32[]{:S(2)}) async-start(f32[32,2,32,256]{3,2,1,0:T(8,128)} %copy.124), calls=%async_computation.2 | async-start | bytes 4194304 | tf_op jit(solution)/shard_map/all_to_all | solution.py:162
  432.6 0.3 reduce-scatter.5.cloned.1.call-start
  432.9 0.4 fusion.88
  433.4 2.0 fusion.38
  435.4 0.0 reduce-scatter.5.cloned.1.call-update
  435.4 0.1 copy.120
  435.6 0.1 reshape.227
  435.7 0.4 fusion.41
  436.1 5.1 %gather_fusion = f32[768]{0:T(1024)S(1)} fusion(f32[128,64]{0,1:T(8,128)S(1)} %fusion.41, s32[768]{0:T(1024)S(1)} %reshape.227), kind=kCustom, calls=%fused_computation | custom fusion | bytes 12288 | tf_op jit(solution)/shard_map/jit(take_along_axis)/gather | solution.py:132
  441.2 0.1 reshape.230
  441.4 0.1 copy.121
  441.5 1.8 select_reduce_fusion
  443.3 25.9 %reduce-scatter.5.cloned.1.call-done = f32[128,256]{1,0:T(8,128)} async-done(((f32[128,2048]{1,0:T(8,128)}), f32[128,256]{1,0:T(8,128)}) %reduce-scatter.5.cloned.1.call-update) | async-done | bytes 131088 | tf_op jit(solution)/shard_map/reduce_scatter | solution.py:166
  469.2 12.7 %all-to-all-done.1 = f32[32,2,32,256]{3,2,1,0:T(8,128)} async-done(((f32[32,2,32,256]{3,2,1,0:T(8,128)}), f32[32,2,32,256]{3,2,1,0:T(8,128)}, u32[]{:S(2)}, u32[]{:S(2)}) %all-to-all-start.1) | async-done | bytes 2097184 | tf_op jit(solution)/shard_map/all_to_all | solution.py:162
  481.9 4.3 fusion.33
  (51 shorter events, 0.3 us)
Async XLA Ops:
  7.2 32.9 %copy-start = (bf16[2048,384]{1,0:T(8,128)(2,1)S(1)}, bf16[2048,384]{1,0:T(8,128)(2,1)}, u32[]{:S(2)}) copy-start(bf16[2048,384]{1,0:T(8,128)(2,1)} %param.24) | copy-start | bytes 4718596
  7.2 31.7 %copy-start.12 = (bf16[512]{0:T(512)(128)(2,1)S(1)}, bf16[512]{0:T(512)(128)(2,1)}, u32[]{:S(2)}) copy-start(bf16[512]{0:T(512)(128)(2,1)} %param.26) | copy-start | bytes 3076
  7.2 31.7 %copy-start.11 = (s32[128]{0:T(128)S(1)}, s32[128]{0:T(128)}, u32[]{:S(2)}) copy-start(s32[128]{0:T(128)} %param.20) | copy-start | bytes 1540
  7.2 98.0 %all-gather.3.cloned.1.call-start = ((), (), s32[]{:S(2)}) async-start(), calls=%async_computation.6 | async-start | bytes 9437184 | tf_op jit(solution)/shard_map/all_gather | solution.py:123
  39.4 1.7 copy-start.8
  39.7 2.1 copy-start.7
  45.0 1.4 copy-start.3
  45.0 1.9 copy-start.15
  46.9 3.5 copy-start.4
  50.4 1.5 copy-start.9
  50.4 4.4 copy-start.10
  51.8 367.8 %reduce-scatter.3.cloned.1.call-start = ((), (), s32[]{:S(2)}) async-start(), calls=%async_computation.4 | async-start | bytes 18874368 | tf_op jit(solution)/shard_map/reduce_scatter | solution.py:156
  112.1 195.4 %copy-start.13 = (bf16[2,2048,176]{1,2,0:T(8,128)(2,1)S(1)}, bf16[2,2048,176]{1,2,0:T(8,128)(2,1)}, u32[]{:S(2)}) copy-start(bf16[2,2048,176]{1,2,0:T(8,128)(2,1)} %param.32) | copy-start | bytes 4325380
  304.2 3.2 copy-start.2
  422.8 10.1 %copy-start.14 = (bf16[2048,176]{0,1:T(8,128)(2,1)S(1)}, bf16[2048,176]{0,1:T(8,128)(2,1)}, u32[]{:S(2)}) copy-start(bf16[2048,176]{0,1:T(8,128)(2,1)} %param.35) | copy-start | bytes 2162692
  422.8 10.5 %copy-start.5 = (bf16[176,2048]{1,0:T(8,128)(2,1)S(1)}, bf16[176,2048]{1,0:T(8,128)(2,1)}, u32[]{:S(2)}) copy-start(bf16[176,2048]{1,0:T(8,128)(2,1)} %param.37) | copy-start | bytes 2162692
  422.8 10.5 %copy-start.6 = (bf16[2048,176]{0,1:T(8,128)(2,1)S(1)}, bf16[2048,176]{0,1:T(8,128)(2,1)}, u32[]{:S(2)}) copy-start(bf16[2048,176]{0,1:T(8,128)(2,1)} %param.36) | copy-start | bytes 2162692
  422.9 59.1 %all-to-all-start.1 = ((f32[32,2,32,256]{3,2,1,0:T(8,128)}), f32[32,2,32,256]{3,2,1,0:T(8,128)}, u32[]{:S(2)}, u32[]{:S(2)}) async-start(f32[32,2,32,256]{3,2,1,0:T(8,128)} %copy.124), calls=%async_computation.2 | async-start | bytes 4194304 | tf_op jit(solution)/shard_map/all_to_all | solution.py:162
  432.6 36.6 %reduce-scatter.5.cloned.1.call-start = ((), (), s32[]{:S(2)}) async-start(), calls=%async_computation.5 | async-start | bytes 1179648 | tf_op jit(solution)/shard_map/reduce_scatter | solution.py:166
  433.4 2.3 copy-start.16
  441.5 44.8 %copy-start.1 = (bf16[2048,384]{1,0:T(8,128)(2,1)S(1)}, bf16[2048,384]{1,0:T(8,128)(2,1)}, u32[]{:S(2)}) copy-start(bf16[2048,384]{1,0:T(8,128)(2,1)} %param.24) | copy-start | bytes 4718596
Sparse Core Ops, SparseCore 0:
  52.0 53.2 all-gather.2
  326.6 92.9 reduce-scatter.2
  436.0 33.1 reduce-scatter.4
